TPU v7x, 512 devices: a whole 4x4x16 slice. The times are simulated.
512 devices in a mesh: chan: 32 (over z, x_hi), seg: 16 (over y, x_lo, core).
Axes of the slice: x: 4 (x_hi: 2, x_lo: 2; x = x_hi * 2 + x_lo), y: 4, z: 16, core: 2. Of those that a mesh axis runs over, the one named last changes fastest.
Arguments:
- traces: bfloat16 [512, 16, 384], P('chan', 'seg')
- taper_len: int32 [512], P('chan'), may hold values from 1 to 192
- gather_id: int32 [512, 512], P('chan'), may hold values from 0 to 511, as said below
- offset_bin: int32 [512, 512], P('chan'), may hold values from 0 to 1, as said below
Outputs:
- stack: float32 [512, 2, 256], P(('chan', 'seg'))
Inputs may be any that keep to these rules, and one draw needn't show every extreme that they name: Channels lie on a fiber at integer positions p_0 < p_1 < ... with steps of 2 to 5; gather_id[i, j] = floor((p_i + p_j - 2 p_0) * 512 / (2 (p_last - p_0) + 1)). offset_bin[i, j] = floor(|p_i - p_j| * 2 / (p_last - p_0 + 1)) with the same positions.
All inputs are finite; a program needn't handle non-finite values.
Results may differ from a plain program's by a relative error of at most 0.0039.
Values may be sent and summed in bfloat16 or wider, within the bound.
No kernel may reach another device: no remote copies, remote signals or barrier semaphores. Data moves between devices by JAX's collectives and lax.ppermute only.
A program may use at most 64 MiB of HBM per device.

v0:
```python
import math
import jax
import jax.numpy as jnp
from jax import lax
from jax.sharding import PartitionSpec as P

LAGS = 256
OFFBINS = 2


def normalize(traces, taper_len):
    values = traces.astype(jnp.float32)
    sample_count = values.shape[2]
    power = jnp.mean(values * values, axis=2, keepdims=True)
    times = jnp.arange(sample_count).astype(jnp.float32)
    length = taper_len.astype(jnp.float32)[:, None, None]
    window = jnp.minimum(1.0, jnp.minimum((times + 1.0) / length, (sample_count - times) / length))
    return (window * values * lax.rsqrt(power + 1e-06)).astype(jnp.bfloat16)


def hankel(normed, lag_count):
    chan_count, seg_count, sample_count = normed.shape
    turned = jnp.transpose(normed, (1, 2, 0))
    padded = jnp.pad(turned, ((0, 0), (lag_count // 2, lag_count // 2), (0, 0)))
    slices = [padded[:, lag_count - k : lag_count - k + sample_count, :] for k in range(lag_count)]
    picked = jnp.stack(slices, axis=3)
    return picked.reshape(seg_count * sample_count, chan_count * lag_count)


def shards(traces, taper_len, gather_id, offset_bin):
    chan_count = traces.shape[0]
    chan_devices = lax.axis_size("chan")
    seg_devices = lax.axis_size("seg")
    bucket_count = chan_devices * seg_devices * OFFBINS
    normed = normalize(traces, taper_len)
    kernel = hankel(normed, LAGS)
    first_row = lax.axis_index("chan") * chan_count
    own_rows = first_row + jnp.arange(chan_count, dtype=jnp.int32)[None, :]
    empty = jnp.zeros((bucket_count, LAGS), jnp.float32)
    piece = lax.all_gather(normed, "chan", axis=0, tiled=True)
    row_count = piece.shape[0]
    product = jnp.dot(piece.reshape(row_count, -1), kernel, preferred_element_type=jnp.float32)
    product = product.reshape(row_count * chan_count, LAGS)
    labels = jnp.transpose(gather_id * OFFBINS + offset_bin)
    partner = jnp.arange(row_count, dtype=jnp.int32)[:, None]
    labels = jnp.where(partner == own_rows, bucket_count, labels).reshape(-1)
    total = empty.at[labels].add(product, mode="drop")
    scale = 1.0 / math.sqrt(traces.shape[2] * traces.shape[1] * seg_devices)
    stacked = (total * scale).reshape(chan_devices * seg_devices, OFFBINS, LAGS)
    result = lax.psum_scatter(stacked, ("chan", "seg"), scatter_dimension=0, tiled=True)
    return result


def solution(mesh):
    placed = (P("chan", "seg", None), P("chan"), P("chan", None), P("chan", None))
    return jax.shard_map(
        shards,
        mesh=mesh,
        in_specs=placed,
        out_specs=P(("chan", "seg"), None, None),
        check_vma=False,
    )
```

profile of v0, /device:TPU:1, one launch (start us, length us, event | category | flops | bytes accessed | tf_op | source)
XLA Modules:
  0.0 647.5 jit_solution(15832972223417551559)
XLA Ops:
  6.5 0.9 fusion.7
  7.4 0.7 convert_element_type.24
  8.1 0.8 fusion.264
  8.9 0.8 fusion.6
  10.2 0.1 constant_dynamic-update-slice_fusion.248
  10.3 0.1 constant_dynamic-update-slice_fusion.247
  10.4 0.1 constant_dynamic-update-slice_fusion.246
  10.4 0.1 constant_dynamic-update-slice_fusion.245
  10.5 0.1 constant_dynamic-update-slice_fusion.244
  10.6 0.1 constant_dynamic-update-slice_fusion.243
  10.7 0.1 constant_dynamic-update-slice_fusion.242
  10.8 0.1 constant_dynamic-update-slice_fusion.241
  20.1 0.1 constant_dynamic-update-slice_fusion.127
  30.5 0.8 copy.264
  31.3 71.5 %all_gather.3 = bf16[512,1,384]{2,0,1:T(8,128)(2,1)S(1)} all-gather(bf16[16,1,384]{2,0,1:T(8,128)(2,1)S(1)} %fusion.6), channel_id=1, replica_groups=mesh['chan'=32,'seg'=16] {'chan'}, dimensions={0}, use_global_device_ids=true | all-gather | bytes 405504 | tf_op jit(solution)/shard_map/all_gather | solution.py:40
  102.8 5.6 fusion.2
  108.4 9.3 %reshape.172 = f32[8192,256]{1,0:T(8,128)} reshape(f32[512,4096]{1,0:T(8,128)} %fusion.2) | data formatting | bytes 16777216 | tf_op jit(solution)/shard_map/reshape | solution.py:43
  117.8 0.1 copy.263
  117.9 0.2 reshape.163
  118.1 44.9 %scatter_custom_fusion = f32[1024,256]{1,0:T(8,128)S(1)} fusion(s32[8192]{0:T(1024)S(1)} %bitcast.1034, f32[8192,256]{1,0:T(8,128)} %reshape.172, f32[]{:T(128)} %constant.13.clone.1), kind=kCustom, calls=%fused_computation.258 | custom fusion | flops 2097152 | bytes 1049088 | tf_op jit(solution)/shard_map/scatter-add | solution.py:47
  163.0 0.1 broadcast_multiply_fusion
  163.1 1.7 reshape.167
  164.7 474.7 %all-reduce.4.cloned.1.call-done = f32[512,2,256]{2,1,0:T(2,128)} async-done(((f32[512,2,256]{2,1,0:T(2,128)}), f32[512,2,256]{2,1,0:T(2,128)}) %all-reduce.4.cloned.1.call-update) | async-done | bytes 1048592
  639.4 1.2 constant_dynamic-slice_fusion
  (260 shorter events, 20.1 us)
Async XLA Ops:
  6.5 13.5 %copy-start = (bf16[16,1,384]{2,0,1:T(8,128)(2,1)S(1)}, bf16[16,1,384]{2,0,1:T(8,128)(2,1)}, u32[]{:S(2)}) copy-start(bf16[16,1,384]{2,0,1:T(8,128)(2,1)} %param.4) | copy-start | bytes 36868
  6.5 632.9 %all-reduce.4.cloned.1.call-start = ((), (), s32[]{:S(2)}) async-start(), calls=%async_computation | async-start | bytes 2097152
  108.4 9.3 %copy-start.1 = (s32[16,512]{1,0:T(8,128)S(1)}, s32[16,512]{1,0:T(8,128)}, u32[]{:S(2)}) copy-start(s32[16,512]{1,0:T(8,128)} %param.7) | copy-start | bytes 98308
  108.4 9.3 %copy-start.2 = (s32[16,512]{1,0:T(8,128)S(1)}, s32[16,512]{1,0:T(8,128)}, u32[]{:S(2)}) copy-start(s32[16,512]{1,0:T(8,128)} %param.6) | copy-start | bytes 98308
Sparse Core Ops, SparseCore 0:
  164.9 474.5 all-reduce.3
where the time goes:
time: 648 us
  waiting for transfers between devices  475 us (73%)
  blocking collectives  71.5 us (11%)
  other arithmetic  48.3 us (7%)
  local copies, waits for them, and re-layouts  33.8 us (5%)
  between operations  13.6 us (2%)
    unnamed x2, waiting for transfers between devices  475 us
    all_gather x1, blocking collectives, shards(): piece = lax.all_gather(normed, 'chan', axis=0, tiled=True)  71.5 us
    scatter-add x1, other arithmetic, shards(): total = empty.at[labels].add(product, mode='drop')  44.9 us
    unnamed x261, local copies, waits for them, and re-layouts  21.8 us
  transfers between devices with their start and end apart: 1, of which 1 were waited for; matrix products, arithmetic and copies ran while one was open for 0% of the time, Pallas kernels for 0%

commit v1 on v0

--- a/solution.py
+++ b/solution.py
@@ -1,3 +1,4 @@
+import functools
 import math
 import jax
 import jax.numpy as jnp
@@ -6,6 +7,16 @@
 
 LAGS = 256
 OFFBINS = 2
+
+
+def place_ranges(x_in, device_axis, which_dim):
+    frame_out = lax.axis_size(device_axis)
+    u1 = jnp.stack(frame_out * [x_in])
+    last = lax.all_to_all(u1, device_axis, split_axis=0, concat_axis=0)
+    return jnp.concatenate(last, axis=which_dim)
+
+
+watch_goods = functools.partial(place_ranges, device_axis="chan", which_dim=0)
 
 
 def normalize(traces, taper_len):
@@ -37,7 +48,7 @@
     first_row = lax.axis_index("chan") * chan_count
     own_rows = first_row + jnp.arange(chan_count, dtype=jnp.int32)[None, :]
     empty = jnp.zeros((bucket_count, LAGS), jnp.float32)
-    piece = lax.all_gather(normed, "chan", axis=0, tiled=True)
+    piece = watch_goods(normed)
     row_count = piece.shape[0]
     product = jnp.dot(piece.reshape(row_count, -1), kernel, preferred_element_type=jnp.float32)
     product = product.reshape(row_count * chan_count, LAGS)

time: 648 us -> 596 us (0.920)
  blocking collectives: 71.5 us -> 0 us
  starting transfers between devices: 0.01 us -> 18.5 us
  waiting for transfers between devices: 475 us -> 468 us
    all_gather x1 -> x0, blocking collectives: 71.5 us -> none  [shards(): piece = lax.all_gather(normed, 'chan', axis=0, tiled=True)]
    all_to_all x0 -> x1, starting transfers between devices: none -> 18.5 us  [place_ranges(): last = lax.all_to_all(u1, device_axis, split_axis=0, concat_axis=0)]
    unnamed x261 -> x257, local copies, waits for them, and re-layouts: 21.8 us -> 21.7 us
  transfers between devices with their start and end apart: 1 -> 2, of which waited for: 1 -> 1; matrix products, arithmetic and copies ran while one was open for 0% -> 5% of each run, Pallas kernels for 0% -> 0%
where the time goes in v1:
time: 596 us; the launch traced here: 595 us
  waiting for transfers between devices  468 us (79%)
  other arithmetic  51 us (9%)
  local copies, waits for them, and re-layouts  37.6 us (6%)
  starting transfers between devices  18.5 us (3%)
  between operations  13.6 us (2%)
    unnamed x2, waiting for transfers between devices  468 us
    scatter-add x1, other arithmetic, shards(): total = empty.at[labels].add(product, mode='drop')  44.9 us
    unnamed x257, local copies, waits for them, and re-layouts  21.7 us
    all_to_all x1, starting transfers between devices, place_ranges(): last = lax.all_to_all(u1, device_axis, split_axis=0, concat_axis=0)  18.5 us
  transfers between devices with their start and end apart: 2, of which 1 were waited for; matrix products, arithmetic and copies ran while one was open for 5% of the time, Pallas kernels for 0%

profile of v1, /device:TPU:1, one launch (start us, length us, event | category | flops | bytes accessed | tf_op | source)
XLA Modules:
  0.0 594.8 jit_solution(4846320762757975763)
XLA Ops:
  6.5 0.9 fusion.5
  7.4 0.7 convert_element_type.26
  8.1 0.8 fusion.265
  8.9 0.8 stack.806
  9.7 18.5 %all-to-all-start = ((bf16[32,16,1,384]{3,1,2,0:T(8,128)(2,1)}), bf16[32,16,1,384]{3,1,2,0:T(8,128)(2,1)S(1)}, u32[]{:S(2)}, u32[]{:S(2)}) async-start(bf16[32,16,1,384]{3,1,2,0:T(8,128)(2,1)} %stack.806), calls=%async_computation | async-start | bytes 786432 | tf_op jit(solution)/shard_map/all_to_all | solution.py:15
  28.2 0.8 fusion.264
  29.5 0.1 constant_dynamic-update-slice_fusion.248
  29.6 0.1 constant_dynamic-update-slice_fusion.247
  29.7 0.1 constant_dynamic-update-slice_fusion.246
  29.8 0.1 constant_dynamic-update-slice_fusion.245
  30.4 0.1 constant_dynamic-update-slice_fusion.237
  39.4 0.1 constant_dynamic-update-slice_fusion.127
  49.8 0.8 copy.264
  50.6 1.4 bitcast_select_fusion
  52.1 1.6 copy.263
  53.7 1.7 reshape.163
  55.4 1.4 compare_select_fusion
  56.7 5.6 fusion.261
  62.3 9.3 %reshape.171 = f32[8192,256]{1,0:T(8,128)} reshape(f32[512,4096]{1,0:T(8,128)} %fusion.261) | data formatting | bytes 16777216 | tf_op jit(solution)/shard_map/reshape | solution.py:54
  71.6 44.9 %scatter_custom_fusion = f32[1024,256]{1,0:T(8,128)S(1)} fusion(s32[8192]{0:T(1024)} %bitcast.1036, f32[8192,256]{1,0:T(8,128)} %reshape.171, f32[]{:T(128)} %constant.13.clone.1), kind=kCustom, calls=%fused_computation.258 | custom fusion | flops 2097152 | bytes 1049088 | tf_op jit(solution)/shard_map/scatter-add | solution.py:58
  116.5 0.1 broadcast_multiply_fusion
  116.6 1.7 reshape.166
  118.3 468.4 %all-reduce.4.cloned.1.call-done = f32[512,2,256]{2,1,0:T(2,128)} async-done(((f32[512,2,256]{2,1,0:T(2,128)}), f32[512,2,256]{2,1,0:T(2,128)}) %all-reduce.4.cloned.1.call-update) | async-done | bytes 1048592
  586.7 1.2 constant_dynamic-slice_fusion
  (258 shorter events, 20.2 us)
Async XLA Ops:
  6.5 32.8 %copy-start = (bf16[16,1,384]{2,0,1:T(8,128)(2,1)S(1)}, bf16[16,1,384]{2,0,1:T(8,128)(2,1)}, u32[]{:S(2)}) copy-start(bf16[16,1,384]{2,0,1:T(8,128)(2,1)} %param.4) | copy-start | bytes 36868
  9.7 47.1 %all-to-all-start = ((bf16[32,16,1,384]{3,1,2,0:T(8,128)(2,1)}), bf16[32,16,1,384]{3,1,2,0:T(8,128)(2,1)S(1)}, u32[]{:S(2)}, u32[]{:S(2)}) async-start(bf16[32,16,1,384]{3,1,2,0:T(8,128)(2,1)} %stack.806), calls=%async_computation | async-start | bytes 786432 | tf_op jit(solution)/shard_map/all_to_all | solution.py:15
  28.2 558.5 %all-reduce.4.cloned.1.call-start = ((), (), s32[]{:S(2)}) async-start(), calls=%async_computation.1 | async-start | bytes 2097152
Sparse Core Ops, SparseCore 0:
  118.4 468.2 all-reduce.3
